TPU v7x, 512 devices: a whole 4x4x16 slice. The times are simulated.
512 devices in a mesh: row: 64 (over z, x), rep: 8 (over y, core).
Axes of the slice: x: 4, y: 4, z: 16, core: 2. Of those that a mesh axis runs over, the one named last changes fastest.
Arguments:
- features: bfloat16 [16384, 128], P('row', 'rep'), may hold values from -6 to 6
- owner_index: int32 [16384], P('row'), may hold values from 0 to 16383, as said below
- block_cols: int32 [128, 64], P('row', 'rep'), may hold values from 0 to 127, as said below
- block_count: int32 [128], P('row'), may hold values from 1 to 64, as said below
- tiles: bfloat16 [128, 64, 128, 128], P('row', 'rep'), may hold values from -0.109375 to 0.109375
- weight: bfloat16 [128, 256], P(None, 'rep'), may hold values from -0.75 to 0.75
- bias: float32 [256], P('rep'), may hold values from -4 to 4
- grad_out: bfloat16 [16384, 256], P('row', 'rep'), may hold values from -6 to 6
Outputs:
- hidden: bfloat16 [16384, 256], P('row', 'rep')
- weight_grad: float32 [128, 256], P(None, 'rep')
- bias_grad: float32 [256], P('rep')
Inputs may be any that keep to these rules, and one draw needn't show every extreme that they name: `owner_index`: A permutation; the 256 rows of each loader shard hold exactly 4 positions of every partition's 2*128 rows. `block_cols`: the block columns of one block row are distinct. Block column c belongs to partition c // 2. Over all slots of one partition's 2 block rows, exactly 1 distinct block columns of each partition are named. `block_count`: some block row has all 64 slots live.
All inputs are finite; a program needn't handle non-finite values.
Results may differ from a plain program's by a relative error of at most 0.017.
Values may be sent and summed in bfloat16 or wider, within the bound.
No kernel may reach another device: no remote copies, remote signals or barrier semaphores. Data moves between devices by JAX's collectives and lax.ppermute only.
A program may use at most 64 MiB of HBM per device.

v0:
```python
import jax
import jax.numpy as jnp
from jax import lax
from jax.sharding import PartitionSpec as P


def sum_over(x, axis_name, count):
    rows = x.shape[0]
    pieces = x.reshape((count, rows // count) + x.shape[1:])
    got = lax.all_to_all(pieces, axis_name, 0, 0, tiled=True)
    reduced = jnp.sum(got.astype(jnp.float32), axis=0)
    return reduced


def spread(x, axis_name, count):
    wide = jnp.broadcast_to(x[None], (count,) + x.shape)
    return lax.all_to_all(wide, axis_name, 0, 0, tiled=True)


def on_device(features, owner_index, block_cols, block_count, tiles, weight, bias, grad_out):
    rows_part, cols_dev = features.shape
    parts = lax.axis_size("row")
    reps = lax.axis_size("rep")
    per_pair = rows_part // parts
    rb, slots_dev, size_blk = (tiles.shape[0], tiles.shape[1], tiles.shape[2])
    destination = owner_index // rows_part
    order = jnp.argsort(destination, stable=True)
    send_rows = features[order]
    send_pos = (owner_index[order] % rows_part).astype(jnp.bfloat16)
    packet = jnp.concatenate([send_rows.T, send_pos[None, :]], axis=0)
    everyone = spread(packet, "row", parts)
    width = cols_dev + 1
    grouped = (
        everyone.reshape(parts, width, parts, per_pair)
        .transpose(2, 1, 0, 3)
        .reshape(parts, width, rows_part)
    )
    pos = grouped[:, cols_dev, :].astype(jnp.int32)
    values = grouped[:, :cols_dev, :]
    cols_all = lax.all_gather(block_cols, "rep", axis=1, tiled=True)
    part_of = cols_all // rb
    half_of = cols_all % rb
    part_ids = jnp.arange(parts, dtype=jnp.int32)
    hit = part_of[None, :, :] == part_ids[:, None, None]
    half = jnp.max(jnp.where(hit, half_of[None, :, :], 0), axis=(1, 2))
    node_ids = jnp.arange(size_blk, dtype=jnp.int32)
    target = half[:, None, None] * size_blk + node_ids[None, None, :]
    pick = (pos[:, :, None] == target).astype(jnp.bfloat16)
    needed = jnp.einsum("qfg,qgn->qfn", values, pick, preferred_element_type=jnp.float32).astype(
        jnp.bfloat16
    )
    peer_parts = part_of.reshape(rb, reps, slots_dev).transpose(1, 0, 2)
    outgoing = needed[peer_parts]
    incoming = lax.all_to_all(outgoing, "rep", 0, 0, tiled=True)
    slot_ids = lax.axis_index("rep") * slots_dev + jnp.arange(slots_dev, dtype=jnp.int32)
    live = slot_ids[None, :] < block_count[:, None]
    tiles_live = jnp.where(live[:, :, None, None], tiles, jnp.zeros_like(tiles))
    partial = jnp.einsum(
        "rsin,jrsfn->rijf", tiles_live, incoming, preferred_element_type=jnp.float32
    )
    partial = partial.reshape(rows_part, reps * cols_dev)
    agg_part = sum_over(partial, "rep", reps).astype(jnp.bfloat16)
    agg = spread(agg_part, "rep", reps).reshape(rows_part, reps * cols_dev)
    pre = jnp.dot(agg, weight, preferred_element_type=jnp.float32) + bias
    hidden = jax.nn.silu(pre).astype(jnp.bfloat16)
    sig = jax.nn.sigmoid(pre)
    dpre = (grad_out.astype(jnp.float32) * sig * (1.0 + pre * (1.0 - sig))).astype(jnp.bfloat16)
    weight_term = jnp.dot(agg.T, dpre, preferred_element_type=jnp.float32)
    bias_term = jnp.sum(dpre.astype(jnp.float32), axis=0)
    flat = jnp.concatenate([weight_term.reshape(-1), bias_term])
    lanes = 128
    chunk = lanes * -(-flat.shape[0] // (parts * lanes))
    flat = jnp.pad(flat, (0, parts * chunk - flat.shape[0])).reshape(parts, chunk)
    total = spread(sum_over(flat, "row", parts), "row", parts).reshape(-1)
    n_w = weight_term.size
    weight_grad = total[:n_w].reshape(weight_term.shape)
    bias_grad = total[n_w : n_w + bias_term.shape[0]]
    return (hidden, weight_grad, bias_grad)


def solution(mesh):
    placed = (
        P("row", "rep"),
        P("row"),
        P("row", "rep"),
        P("row"),
        P("row", "rep", None, None),
        P(None, "rep"),
        P("rep"),
        P("row", "rep"),
    )
    return jax.shard_map(
        on_device,
        mesh=mesh,
        in_specs=placed,
        out_specs=(P("row", "rep"), P(None, "rep"), P("rep")),
        check_vma=False,
    )
```

profile of v0, /device:TPU:8, one launch (start us, length us, event | category | flops | bytes accessed | tf_op | source)
XLA Modules:
  0.0 153.3 jit_solution(980085118121361113)
XLA Ops:
  0.6 0.0 copy-start
  0.6 0.7 and_select_fusion.3
  1.3 3.2 %sort.17 = (s32[256]{0:T(256)}, s32[256]{0:T(256)S(1)}) sort(s32[256]{0:T(256)S(1)} %and_select_fusion.3, s32[256]{0:T(256)S(1)} %iota.22), dimensions={0}, to_apply=%region_0.1 | sort | flops 2048 | bytes 4096 | tf_op jit(solution)/shard_map/jit(argsort)/sort | solution.py:27
  4.5 2.0 %gather_fusion.1 = s32[256]{0:T(256)S(1)} fusion(s32[256]{0:T(256)} %param.9, s32[1024]{0:T(1024)S(1)} %pad_clamp_fusion.1), kind=kCustom, calls=%fused_computation.1 | custom fusion | bytes 3072 | tf_op jit(solution)/shard_map/gather | solution.py:29
  6.5 0.8 copy.76
  7.3 0.9 gather_fusion
  8.2 0.1 copy.77
  8.3 0.0 copy-start.1
  8.3 0.9 broadcast_in_dim.35
  9.2 18.6 %all-to-all-start = ((bf16[64,17,256]{2,1,0:T(8,128)(2,1)}), bf16[64,17,256]{2,1,0:T(8,128)(2,1)S(1)}, u32[]{:S(2)}, u32[]{:S(2)}) async-start(bf16[64,17,256]{2,1,0:T(8,128)(2,1)} %broadcast_in_dim.35), calls=%async_computation | async-start | bytes 1572864 | tf_op jit(solution)/shard_map/all_to_all | solution.py:17
  27.8 0.0 copy-done.1
  27.8 8.8 %all-gather = s32[8,8,2]{1,2,0:T(2,128)S(1)} all-gather(s32[1,8,2]{1,2,0:T(2,128)S(1)} %bitcast.68), channel_id=1, replica_groups=mesh['row'=64,'rep'=8] {'rep'}, dimensions={0}, use_global_device_ids=true | all-gather | bytes 576 | tf_op jit(solution)/shard_map/all_gather | solution.py:40
  36.6 0.1 reshape.183
  36.7 0.1 reshape.148
  36.8 0.1 reshape.172
  36.9 0.1 select_reduce_fusion
  37.0 0.1 iota_add_fusion
  37.1 34.8 %all-to-all-done = bf16[64,17,256]{2,1,0:T(8,128)(2,1)S(1)} async-done(((bf16[64,17,256]{2,1,0:T(8,128)(2,1)}), bf16[64,17,256]{2,1,0:T(8,128)(2,1)S(1)}, u32[]{:S(2)}, u32[]{:S(2)}) %all-to-all-start) | async-done | bytes 557088 | tf_op jit(solution)/shard_map/all_to_all | solution.py:17
  71.8 0.8 copy.78
  72.7 1.7 %copy.79 = bf16[64,17,64,4]{0,3,2,1:T(4,128)(2,1)S(1)} copy(bf16[64,17,64,4]{2,3,0,1:T(4,128)(2,1)S(1)} %bitcast.60) | data formatting | bytes 1114112 | tf_op jit(solution)/shard_map/transpose | solution.py:35
  74.4 0.1 slice.23
  74.5 0.8 copy.96
  75.4 0.1 copy.81
  75.4 3.7 %fusion.4 = bf16[64,16,128]{2,1,0:T(8,128)(2,1)S(1)} fusion(bf16[64,16,256]{2,1,0:T(8,128)(2,1)S(1)} %copy.96, s32[64,128]{1,0:T(8,128)S(1)} %iota_add_fusion, s32[64,256]{1,0:T(8,128)S(1)} %copy.81), kind=kOutput, calls=%fused_computation.7 | convolution fusion | flops 69337088 | bytes 884736 | tf_op jit(solution)/shard_map/qfg,qgn->qfn/dot_general | solution.py:49
  79.1 0.0 copy-start.4
  79.1 0.0 copy-start.2
  79.1 1.5 gather_fusion.2
  80.6 4.9 %all-to-all-start.1 = ((bf16[8,2,8,16,128]{4,3,2,1,0:T(8,128)(2,1)}), bf16[8,2,8,16,128]{4,3,2,1,0:T(8,128)(2,1)S(1)}, u32[]{:S(2)}, u32[]{:S(2)}) async-start(bf16[8,2,8,16,128]{4,3,2,1,0:T(8,128)(2,1)} %bitcast.12), calls=%async_computation.1 | async-start | bytes 1048576 | tf_op jit(solution)/shard_map/all_to_all | solution.py:54
  85.5 0.0 copy-done.4
  85.6 0.1 broadcast_compare_fusion.1
  85.6 8.8 %all-to-all-done.1 = bf16[8,2,8,16,128]{4,3,2,1,0:T(8,128)(2,1)S(1)} async-done(((bf16[8,2,8,16,128]{4,3,2,1,0:T(8,128)(2,1)}), bf16[8,2,8,16,128]{4,3,2,1,0:T(8,128)(2,1)S(1)}, u32[]{:S(2)}, u32[]{:S(2)}) %all-to-all-start.1) | async-done | bytes 524320 | tf_op jit(solution)/shard_map/all_to_all | solution.py:54
  94.4 0.0 copy-done.2
  94.4 0.4 convolution_bitcast_fusion
  94.8 0.0 copy-start.3
  94.8 0.0 copy-start.5
  94.8 0.1 copy.85
  95.0 0.2 reshape_reshape.6
  95.2 0.2 copy.86
  95.4 8.5 %all_to_all.30 = f32[8,32,128]{2,1,0:T(8,128)S(1)} all-to-all(f32[8,32,128]{2,1,0:T(8,128)S(1)} %copy.86), channel_id=1, replica_groups=mesh['row'=64,'rep'=8] {'rep'}, dimensions={0} | all-to-all | bytes 262144 | tf_op jit(solution)/shard_map/all_to_all | solution.py:10
  103.9 8.0 %all_to_all.31 = bf16[8,32,128]{2,1,0:T(8,128)(2,1)S(1)} all-to-all(bf16[8,32,128]{2,1,0:T(8,128)(2,1)S(1)} %broadcast_in_dim.39), channel_id=1, replica_groups=mesh['row'=64,'rep'=8] {'rep'}, dimensions={0} | all-to-all | bytes 131072 | tf_op jit(solution)/shard_map/all_to_all | solution.py:17
  111.9 0.0 copy-done
  111.9 0.0 copy-done.3
  111.9 0.0 copy-done.5
  112.0 0.9 convert_reduce_fusion
  112.8 0.2 fusion.16
  113.0 0.1 reshape.150
  113.1 20.2 %all_to_all.32 = f32[64,1,128]{2,1,0:T(1,128)S(1)} all-to-all(f32[64,1,128]{2,1,0:T(1,128)S(1)} %bitcast.64), channel_id=1, replica_groups=mesh['row'=64,'rep'=8] {'row'}, dimensions={0} | all-to-all | bytes 65536 | tf_op jit(solution)/shard_map/all_to_all | solution.py:10
  133.4 18.6 %all_to_all.33 = f32[64,1,128]{2,1,0:T(1,128)S(1)} all-to-all(f32[64,1,128]{2,1,0:T(1,128)S(1)} %broadcast_in_dim.40), channel_id=1, replica_groups=mesh['row'=64,'rep'=8] {'row'}, dimensions={0} | all-to-all | bytes 65536 | tf_op jit(solution)/shard_map/all_to_all | solution.py:17
  152.0 0.5 slice.26
  152.5 0.1 reshape.151
  152.6 0.7 copy.91
  (19 shorter events, 0.2 us)
Async XLA Ops:
  0.6 111.3 %copy-start = (bf16[128,32]{0,1:T(8,128)(2,1)S(1)}, bf16[128,32]{0,1:T(8,128)(2,1)}, u32[]{:S(2)}) copy-start(bf16[128,32]{0,1:T(8,128)(2,1)} %param.13) | copy-start | bytes 24580
  8.3 19.5 %copy-start.1 = (s32[2,8]{1,0:T(2,128)S(1)}, s32[2,8]{1,0:T(2,128)}, u32[]{:S(2)}) copy-start(s32[2,8]{1,0:T(2,128)} %param.10) | copy-start | bytes 196
  9.2 62.6 %all-to-all-start = ((bf16[64,17,256]{2,1,0:T(8,128)(2,1)}), bf16[64,17,256]{2,1,0:T(8,128)(2,1)S(1)}, u32[]{:S(2)}, u32[]{:S(2)}) async-start(bf16[64,17,256]{2,1,0:T(8,128)(2,1)} %broadcast_in_dim.35), calls=%async_computation | async-start | bytes 1572864 | tf_op jit(solution)/shard_map/all_to_all | solution.py:17
  79.1 6.4 %copy-start.4 = (s32[2]{0:T(128)S(1)}, s32[2]{0:T(128)}, u32[]{:S(2)}) copy-start(s32[2]{0:T(128)} %param.11) | copy-start | bytes 28
  79.1 15.3 %copy-start.2 = (bf16[2,8,128,128]{3,2,1,0:T(8,128)(2,1)S(1)}, bf16[2,8,128,128]{3,2,1,0:T(8,128)(2,1)}, u32[]{:S(2)}) copy-start(bf16[2,8,128,128]{3,2,1,0:T(8,128)(2,1)} %param.12) | copy-start | bytes 1572868
  80.6 13.8 %all-to-all-start.1 = ((bf16[8,2,8,16,128]{4,3,2,1,0:T(8,128)(2,1)}), bf16[8,2,8,16,128]{4,3,2,1,0:T(8,128)(2,1)S(1)}, u32[]{:S(2)}, u32[]{:S(2)}) async-start(bf16[8,2,8,16,128]{4,3,2,1,0:T(8,128)(2,1)} %bitcast.12), calls=%async_computation.1 | async-start | bytes 1048576 | tf_op jit(solution)/shard_map/all_to_all | solution.py:54
  94.8 17.1 %copy-start.3 = (bf16[256,32]{0,1:T(8,128)(2,1)S(1)}, bf16[256,32]{0,1:T(8,128)(2,1)}, u32[]{:S(2)}) copy-start(bf16[256,32]{0,1:T(8,128)(2,1)} %param.15) | copy-start | bytes 49156
  94.8 17.1 %copy-start.5 = (f32[32]{0:T(128)S(1)}, f32[32]{0:T(128)}, u32[]{:S(2)}) copy-start(f32[32]{0:T(128)} %param.14) | copy-start | bytes 388
where the time goes:
time: 154 us; the launch traced here: 153 us
  blocking collectives  64.1 us (42%)
  waiting for transfers between devices  43.6 us (28%)
  starting transfers between devices  23.5 us (15%)
  local copies, waits for them, and re-layouts  11.9 us (8%)
  matrix products  5.13 us (3%)
  other arithmetic  4.26 us (3%)
    all_to_all x1, waiting for transfers between devices, spread(): return lax.all_to_all(wide, axis_name, 0, 0, tiled=True)  34.8 us
    all_to_all x2, blocking collectives, sum_over(): got = lax.all_to_all(pieces, axis_name, 0, 0, tiled=True)  28.8 us
    all_to_all x2, blocking collectives, spread(): return lax.all_to_all(wide, axis_name, 0, 0, tiled=True)  26.5 us
    all_to_all x1, starting transfers between devices, spread(): return lax.all_to_all(wide, axis_name, 0, 0, tiled=True)  18.6 us
    all_to_all x1, waiting for transfers between devices, on_device(): incoming = lax.all_to_all(outgoing, 'rep', 0, 0, tiled=True)  8.81 us
    all_gather x1, blocking collectives, on_device(): cols_all = lax.all_gather(block_cols, 'rep', axis=1, tiled=True)  8.77 us
    all_to_all x1, starting transfers between devices, on_device(): incoming = lax.all_to_all(outgoing, 'rep', 0, 0, tiled=True)  4.92 us
    dot_general x1, matrix products, on_device(): jnp.einsum('qfg,qgn->qfn', values, pick, preferred_element_type=jnp.float32)  3.69 us
  transfers between devices with their start and end apart: 2, of which 2 were waited for; matrix products, arithmetic and copies ran while one was open for 0% of the time, Pallas kernels for 0%

commit v1 on v0

--- a/solution.py
+++ b/solution.py
@@ -2,6 +2,11 @@
 import jax.numpy as jnp
 from jax import lax
 from jax.sharding import PartitionSpec as P
+
+
+def gather_over(block, axis, along):
+    sent = jnp.stack([block] * lax.axis_size(axis))
+    return jnp.concatenate(lax.all_to_all(sent, axis, 0, 0), axis=along)
 
 
 def sum_over(x, axis_name, count):
@@ -37,7 +42,7 @@
     )
     pos = grouped[:, cols_dev, :].astype(jnp.int32)
     values = grouped[:, :cols_dev, :]
-    cols_all = lax.all_gather(block_cols, "rep", axis=1, tiled=True)
+    cols_all = gather_over(block_cols, "rep", 1)
     part_of = cols_all // rb
     half_of = cols_all % rb
     part_ids = jnp.arange(parts, dtype=jnp.int32)

time: 154 us -> 160 us (1.039)
  waiting for transfers between devices: 43.6 us -> 52.7 us
  blocking collectives: 64.1 us -> 55.3 us
  starting transfers between devices: 23.5 us -> 28.3 us
    all_to_all x1, waiting for transfers between devices: 34.8 us -> 43.9 us  [spread(): return lax.all_to_all(wide, axis_name, 0, 0, tiled=True)]
    all_to_all x0 -> x1, starting transfers between devices: none -> 9.07 us  [gather_over(): return jnp.concatenate(lax.all_to_all(sent, axis, 0, 0), axis=along)]
    all_gather x1 -> x0, blocking collectives: 8.77 us -> none  [on_device(): cols_all = lax.all_gather(block_cols, 'rep', axis=1, tiled=True)]
    all_to_all x1, starting transfers between devices: 18.6 us -> 14.4 us  [spread(): return lax.all_to_all(wide, axis_name, 0, 0, tiled=True)]
  transfers between devices with their start and end apart: 2 -> 3, of which waited for: 2 -> 2; matrix products, arithmetic and copies ran while one was open for 0% -> 5% of each run, Pallas kernels for 0% -> 0%
where the time goes in v1:
time: 160 us
  blocking collectives  55.3 us (35%)
  waiting for transfers between devices  52.7 us (33%)
  starting transfers between devices  28.3 us (18%)
  local copies, waits for them, and re-layouts  13.1 us (8%)
  matrix products  5.13 us (3%)
  other arithmetic  4.27 us (3%)
    all_to_all x1, waiting for transfers between devices, spread(): return lax.all_to_all(wide, axis_name, 0, 0, tiled=True)  43.9 us
    all_to_all x2, blocking collectives, sum_over(): got = lax.all_to_all(pieces, axis_name, 0, 0, tiled=True)  28.8 us
    all_to_all x2, blocking collectives, spread(): return lax.all_to_all(wide, axis_name, 0, 0, tiled=True)  26.5 us
    all_to_all x1, starting transfers between devices, spread(): return lax.all_to_all(wide, axis_name, 0, 0, tiled=True)  14.4 us
    all_to_all x1, starting transfers between devices, gather_over(): return jnp.concatenate(lax.all_to_all(sent, axis, 0, 0), axis=along)  9.07 us
    all_to_all x1, waiting for transfers between devices, on_device(): incoming = lax.all_to_all(outgoing, 'rep', 0, 0, tiled=True)  8.81 us
    all_to_all x1, starting transfers between devices, on_device(): incoming = lax.all_to_all(outgoing, 'rep', 0, 0, tiled=True)  4.8 us
    dot_general x1, matrix products, on_device(): jnp.einsum('qfg,qgn->qfn', values, pick, preferred_element_type=jnp.float32)  3.69 us
  transfers between devices with their start and end apart: 3, of which 2 were waited for; matrix products, arithmetic and copies ran while one was open for 5% of the time, Pallas kernels for 0%

profile of v1, /device:TPU:8, one launch (start us, length us, event | category | flops | bytes accessed | tf_op | source)
XLA Modules:
  0.0 159.7 jit_solution(6043022150055757966)
XLA Ops:
  0.6 0.0 copy-start
  0.6 1.3 stack.2
  1.9 9.1 %all-to-all-start.1 = ((s32[8,2,8]{2,1,0:T(2,128)}), s32[8,2,8]{2,1,0:T(2,128)S(1)}, u32[]{:S(2)}, u32[]{:S(2)}) async-start(s32[8,2,8]{2,1,0:T(2,128)} %stack.2), calls=%async_computation.1 | async-start | bytes 16384 | tf_op jit(solution)/shard_map/all_to_all | solution.py:9
  11.0 0.7 and_select_fusion.4
  11.7 3.2 %sort.17 = (s32[256]{0:T(256)}, s32[256]{0:T(256)S(1)}) sort(s32[256]{0:T(256)S(1)} %and_select_fusion.4, s32[256]{0:T(256)S(1)} %iota.22), dimensions={0}, to_apply=%region_0.1 | sort | flops 2048 | bytes 4096 | tf_op jit(solution)/shard_map/jit(argsort)/sort | solution.py:32
  14.9 2.0 %gather_fusion.1 = s32[256]{0:T(256)S(1)} fusion(s32[256]{0:T(256)} %param.9, s32[1024]{0:T(1024)S(1)} %pad_clamp_fusion.1), kind=kCustom, calls=%fused_computation.1 | custom fusion | bytes 3072 | tf_op jit(solution)/shard_map/gather | solution.py:34
  16.9 0.8 copy.71
  17.7 0.9 gather_fusion
  18.5 0.1 copy.72
  18.6 0.0 all-to-all-done.1
  18.6 0.9 broadcast_in_dim.35
  19.6 14.4 %all-to-all-start = ((bf16[64,17,256]{2,1,0:T(8,128)(2,1)}), bf16[64,17,256]{2,1,0:T(8,128)(2,1)S(1)}, u32[]{:S(2)}, u32[]{:S(2)}) async-start(bf16[64,17,256]{2,1,0:T(8,128)(2,1)} %broadcast_in_dim.35), calls=%async_computation | async-start | bytes 1572864 | tf_op jit(solution)/shard_map/all_to_all | solution.py:22
  34.0 0.1 reshape.202
  34.1 0.1 reshape.226
  34.2 0.1 select_reduce_fusion
  34.4 0.1 iota_add_fusion
  34.4 43.9 %all-to-all-done = bf16[64,17,256]{2,1,0:T(8,128)(2,1)S(1)} async-done(((bf16[64,17,256]{2,1,0:T(8,128)(2,1)}), bf16[64,17,256]{2,1,0:T(8,128)(2,1)S(1)}, u32[]{:S(2)}, u32[]{:S(2)}) %all-to-all-start) | async-done | bytes 557088 | tf_op jit(solution)/shard_map/all_to_all | solution.py:22
  78.4 0.8 copy.73
  79.2 1.7 %copy.74 = bf16[64,17,64,4]{0,3,2,1:T(4,128)(2,1)S(1)} copy(bf16[64,17,64,4]{2,3,0,1:T(4,128)(2,1)S(1)} %bitcast.34) | data formatting | bytes 1114112 | tf_op jit(solution)/shard_map/transpose | solution.py:40
  80.9 0.1 slice.23
  81.0 0.8 copy.90
  81.9 0.1 copy.76
  82.0 3.7 %fusion.4 = bf16[64,16,128]{2,1,0:T(8,128)(2,1)S(1)} fusion(bf16[64,16,256]{2,1,0:T(8,128)(2,1)S(1)} %copy.90, s32[64,128]{1,0:T(8,128)S(1)} %iota_add_fusion, s32[64,256]{1,0:T(8,128)S(1)} %copy.76), kind=kOutput, calls=%fused_computation.7 | convolution fusion | flops 69337088 | bytes 884736 | tf_op jit(solution)/shard_map/qfg,qgn->qfn/dot_general | solution.py:54
  85.6 0.0 copy-start.3
  85.6 0.0 copy-start.1
  85.7 1.5 gather_fusion.2
  87.1 4.8 %all-to-all-start.2 = ((bf16[8,2,8,16,128]{4,3,2,1,0:T(8,128)(2,1)}), bf16[8,2,8,16,128]{4,3,2,1,0:T(8,128)(2,1)S(1)}, u32[]{:S(2)}, u32[]{:S(2)}) async-start(bf16[8,2,8,16,128]{4,3,2,1,0:T(8,128)(2,1)} %bitcast.9), calls=%async_computation.2 | async-start | bytes 1048576 | tf_op jit(solution)/shard_map/all_to_all | solution.py:59
  91.9 0.0 copy-done.3
  91.9 0.1 broadcast_compare_fusion.2
  92.0 8.8 %all-to-all-done.2 = bf16[8,2,8,16,128]{4,3,2,1,0:T(8,128)(2,1)S(1)} async-done(((bf16[8,2,8,16,128]{4,3,2,1,0:T(8,128)(2,1)}), bf16[8,2,8,16,128]{4,3,2,1,0:T(8,128)(2,1)S(1)}, u32[]{:S(2)}, u32[]{:S(2)}) %all-to-all-start.2) | async-done | bytes 524320 | tf_op jit(solution)/shard_map/all_to_all | solution.py:59
  100.8 0.0 copy-done.1
  100.8 0.4 convolution_bitcast_fusion
  101.2 0.0 copy-start.2
  101.2 0.0 copy-start.4
  101.2 0.1 copy.79
  101.3 0.2 reshape_reshape.6
  101.6 0.2 copy.80
  101.8 8.5 %all_to_all.35 = f32[8,32,128]{2,1,0:T(8,128)S(1)} all-to-all(f32[8,32,128]{2,1,0:T(8,128)S(1)} %copy.80), channel_id=1, replica_groups=mesh['row'=64,'rep'=8] {'rep'}, dimensions={0} | all-to-all | bytes 262144 | tf_op jit(solution)/shard_map/all_to_all | solution.py:15
  110.3 8.0 %all_to_all.36 = bf16[8,32,128]{2,1,0:T(8,128)(2,1)S(1)} all-to-all(bf16[8,32,128]{2,1,0:T(8,128)(2,1)S(1)} %broadcast_in_dim.39), channel_id=1, replica_groups=mesh['row'=64,'rep'=8] {'rep'}, dimensions={0} | all-to-all | bytes 131072 | tf_op jit(solution)/shard_map/all_to_all | solution.py:22
  118.3 0.0 copy-done
  118.3 0.0 copy-done.2
  118.3 0.0 copy-done.4
  118.4 0.9 convert_reduce_fusion
  119.2 0.2 fusion.16
  119.4 0.1 reshape.204
  119.5 20.2 %all_to_all.37 = f32[64,1,128]{2,1,0:T(1,128)S(1)} all-to-all(f32[64,1,128]{2,1,0:T(1,128)S(1)} %bitcast.38), channel_id=1, replica_groups=mesh['row'=64,'rep'=8] {'row'}, dimensions={0} | all-to-all | bytes 65536 | tf_op jit(solution)/shard_map/all_to_all | solution.py:15
  139.8 18.6 %all_to_all.38 = f32[64,1,128]{2,1,0:T(1,128)S(1)} all-to-all(f32[64,1,128]{2,1,0:T(1,128)S(1)} %broadcast_in_dim.40), channel_id=1, replica_groups=mesh['row'=64,'rep'=8] {'row'}, dimensions={0} | all-to-all | bytes 65536 | tf_op jit(solution)/shard_map/all_to_all | solution.py:22
  158.4 0.5 slice.26
  158.9 0.1 reshape.205
  159.0 0.7 copy.85
  (18 shorter events, 0.2 us)
Async XLA Ops:
  0.6 117.7 %copy-start = (bf16[128,32]{0,1:T(8,128)(2,1)S(1)}, bf16[128,32]{0,1:T(8,128)(2,1)}, u32[]{:S(2)}) copy-start(bf16[128,32]{0,1:T(8,128)(2,1)} %param.13) | copy-start | bytes 24580
  1.9 16.7 %all-to-all-start.1 = ((s32[8,2,8]{2,1,0:T(2,128)}), s32[8,2,8]{2,1,0:T(2,128)S(1)}, u32[]{:S(2)}, u32[]{:S(2)}) async-start(s32[8,2,8]{2,1,0:T(2,128)} %stack.2), calls=%async_computation.1 | async-start | bytes 16384 | tf_op jit(solution)/shard_map/all_to_all | solution.py:9
  19.6 58.8 %all-to-all-start = ((bf16[64,17,256]{2,1,0:T(8,128)(2,1)}), bf16[64,17,256]{2,1,0:T(8,128)(2,1)S(1)}, u32[]{:S(2)}, u32[]{:S(2)}) async-start(bf16[64,17,256]{2,1,0:T(8,128)(2,1)} %broadcast_in_dim.35), calls=%async_computation | async-start | bytes 1572864 | tf_op jit(solution)/shard_map/all_to_all | solution.py:22
  85.6 6.3 %copy-start.3 = (s32[2]{0:T(128)S(1)}, s32[2]{0:T(128)}, u32[]{:S(2)}) copy-start(s32[2]{0:T(128)} %param.11) | copy-start | bytes 28
  85.6 15.2 %copy-start.1 = (bf16[2,8,128,128]{3,2,1,0:T(8,128)(2,1)S(1)}, bf16[2,8,128,128]{3,2,1,0:T(8,128)(2,1)}, u32[]{:S(2)}) copy-start(bf16[2,8,128,128]{3,2,1,0:T(8,128)(2,1)} %param.12) | copy-start | bytes 1572868
  87.1 13.7 %all-to-all-start.2 = ((bf16[8,2,8,16,128]{4,3,2,1,0:T(8,128)(2,1)}), bf16[8,2,8,16,128]{4,3,2,1,0:T(8,128)(2,1)S(1)}, u32[]{:S(2)}, u32[]{:S(2)}) async-start(bf16[8,2,8,16,128]{4,3,2,1,0:T(8,128)(2,1)} %bitcast.9), calls=%async_computation.2 | async-start | bytes 1048576 | tf_op jit(solution)/shard_map/all_to_all | solution.py:59
  101.2 17.1 %copy-start.2 = (bf16[256,32]{0,1:T(8,128)(2,1)S(1)}, bf16[256,32]{0,1:T(8,128)(2,1)}, u32[]{:S(2)}) copy-start(bf16[256,32]{0,1:T(8,128)(2,1)} %param.15) | copy-start | bytes 49156
  101.2 17.1 %copy-start.4 = (f32[32]{0:T(128)S(1)}, f32[32]{0:T(128)}, u32[]{:S(2)}) copy-start(f32[32]{0:T(128)} %param.14) | copy-start | bytes 388
